TPU v7x, 512 devices: a whole 4x8x8 slice. The times are simulated.
512 devices in a mesh: dp: 16 (over y, core), cell: 32 (over x, z).
Axes of the slice: x: 4, y: 8, z: 8, core: 2. Of those that a mesh axis runs over, the one named last changes fastest.
Arguments:
- sensitivity: bfloat16 [2048, 200704], P('dp', 'cell'), may hold values from -0.0390625 to 0.0390625
- direction: bfloat16 [16, 200704], P(None, 'cell'), may hold values from -6 to 6
- depth_weight: float32 [200704], P('cell'), may hold values from 0.3 to 3
- counts: int32 [32], P('cell'), may hold values from 4704 to 6272, as said below
- send_lists: int32 [32, 2, 128], P('cell'), may hold values from 0 to 6271, as said below
- neighbours: int32 [6, 200704], P(None, 'cell'), may hold values from 0 to 6528, as said below
Outputs:
- product: float32 [16, 200704], P(None, 'cell')
Inputs may be any that keep to these rules, and one draw needn't show every extreme that they name: `counts`: every partition has at least 4704 live cells; some partition is full in every draw. `send_lists`: entries are local indices of live cells of their own partition. `neighbours`: entries below 6272 are live local cells that differ from the cell's own local index by at most 64; 6272 to 6527 name received rim cells; 6528 is an absent face; padded slots hold only absent faces.
All inputs are finite; a program needn't handle non-finite values.
Results may differ from a plain program's by a relative error of at most 0.0008.
Values sent between devices are 32-bit elements; how exact they have to be, the bound alone decides.
No kernel may reach another device: no remote copies, remote signals or barrier semaphores. Data moves between devices by JAX's collectives and lax.ppermute only.
A program may use at most 64 MiB of HBM per device.

v0:
```python
import jax
import jax.numpy as jnp
from jax import lax
from jax.sharding import PartitionSpec as P


def padded_2(value, sides, width):
    for axis, dim in sides:
        count, length = (lax.axis_size(axis), value.shape[dim])
        up = [(i, (i + 1) % count) for i in range(count - 1)]
        down = [(j, i) for i, j in up]
        last = lax.slice_in_dim(value, length - width, length, axis=dim)
        leading = lax.slice_in_dim(value, 0, width, axis=dim)
        before = lax.ppermute(last, axis, up)
        after = lax.ppermute(leading, axis, down)
        value = jnp.concatenate([before, value, after], axis=dim)
    return value


def butterfly_sum(value, axis):
    count = lax.axis_size(axis)
    rounds = []
    step = 1
    while step < count:
        pairs = [(j, j ^ step) for j in range(count)]
        value = value + lax.ppermute(value, axis, pairs)
        rounds.append(value)
        step *= 2
    return value, rounds


def halving_sum(value, axis):
    count = lax.axis_size(axis)
    me = lax.axis_index(axis)
    steps = []
    step = 1
    while step < count:
        steps.append(step)
        step *= 2
    for step in steps:
        half = value.shape[0] // 2
        low, high = value[:half], value[half:]
        upper = (me & step) != 0
        keep = jnp.where(upper, high, low)
        send = jnp.where(upper, low, high)
        pairs = [(j, j ^ step) for j in range(count)]
        value = keep + lax.ppermute(send, axis, pairs)
    for step in reversed(steps):
        pairs = [(j, j ^ step) for j in range(count)]
        other = lax.ppermute(value, axis, pairs)
        upper = (me & step) != 0
        low = jnp.where(upper, other, value)
        high = jnp.where(upper, value, other)
        value = jnp.concatenate([low, high], axis=0)
    return value


def exchange_sum(value, axis):
    count = lax.axis_size(axis)
    rows = value.shape[0] // count
    pieces = value.reshape(count, rows, value.shape[1])
    pieces = lax.all_to_all(pieces, axis, 0, 0)
    total = pieces[0]
    for source in range(1, count):
        total = total + pieces[source]
    return lax.all_gather(total, axis, axis=0, tiled=True)


def pick_block():
    block_len = 8
    for candidate in range(128, 7, -8):
        block_len = candidate
        break
    return block_len


def pick_group(block_count):
    group_len = 1
    for candidate in range(1, 9):
        if block_count % candidate == 0:
            group_len = candidate
    return group_len


def smoothness(masked_f, weight, send_lists, neighbours, width, gates):
    slots = masked_f.shape[1]
    values = jnp.concatenate([masked_f * weight[None, :], weight[None, :]], axis=0)
    lanes = values.shape[0]
    high = lax.reduce_precision(values, exponent_bits=8, mantissa_bits=7)
    rest = values - high
    middle = lax.reduce_precision(rest, exponent_bits=8, mantissa_bits=7)
    low = rest - middle
    split = jnp.concatenate([high, middle, low], axis=0).astype(jnp.bfloat16)
    rim_index, _ = lax.optimization_barrier((send_lists[0], gates[0]))
    chosen = jnp.arange(slots, dtype=jnp.int32)[:, None] == rim_index.reshape(1, -1)
    chosen_parts = jnp.dot(split, chosen.astype(jnp.bfloat16), preferred_element_type=jnp.float32)
    picked = chosen_parts[:lanes] + chosen_parts[lanes : 2 * lanes] + chosen_parts[2 * lanes :]
    rim = picked.shape[1] // 2
    padded = padded_2(picked, (("cell", 1),), rim)
    rim_vals = jnp.concatenate([padded[:, :rim], padded[:, 3 * rim :]], axis=1)
    rim_high = lax.reduce_precision(rim_vals, exponent_bits=8, mantissa_bits=7)
    rim_rest = rim_vals - rim_high
    rim_middle = lax.reduce_precision(rim_rest, exponent_bits=8, mantissa_bits=7)
    rim_split = jnp.concatenate([rim_high, rim_middle, rim_rest - rim_middle], axis=0)
    rim_split = rim_split.astype(jnp.bfloat16)
    block_len = pick_block()
    block_count = width // block_len
    pieces = 1 + (128 + block_len - 1) // block_len
    spread = jnp.pad(split, ((0, 0), (64, pieces * block_len)))
    local_vals = lax.slice_in_dim(spread, 0, (block_count + pieces - 1) * block_len, axis=1)
    shifted = [
        local_vals[:, m * block_len : (m + block_count) * block_len].reshape(
            3 * lanes, block_count, block_len
        )
        for m in range(pieces)
    ]
    rim_part = jnp.broadcast_to(rim_split[:, None, :], (3 * lanes, block_count, 2 * rim))
    windows = jnp.concatenate(shifted + [rim_part], axis=2).transpose(1, 0, 2)
    span = windows.shape[2]
    position = jnp.arange(width, dtype=jnp.int32)
    anchor = position // block_len * block_len
    column = jnp.where(
        neighbours < slots,
        neighbours - anchor[None, :] + 64,
        jnp.where(neighbours < slots + 2 * rim, pieces * block_len + neighbours - slots, -1),
    )
    column = column.reshape(neighbours.shape[0], block_count, block_len).transpose(1, 0, 2)
    group_len = pick_group(block_count)
    group_count = block_count // group_len
    sums = []
    for g in range(group_count):
        window_set = windows[g * group_len : (g + 1) * group_len]
        column_set = column[g * group_len : (g + 1) * group_len]
        gate = gates[min(g, len(gates) - 1)]
        target = jnp.arange(span, dtype=jnp.int32)[None, None, :, None]
        with jax.named_scope("late_counts" if g >= len(gates) - 1 else f"counts_{g}"):
            column_set, _ = lax.optimization_barrier((column_set, gate))
            hits = jnp.sum((column_set[:, :, None, :] == target).astype(jnp.float32), axis=1)
            hits = hits.astype(jnp.bfloat16)
            part = jnp.einsum(
                "grw,gwb->grb", window_set, hits, preferred_element_type=jnp.float32
            )
        sums.append(part[:, :lanes] + part[:, lanes : 2 * lanes] + part[:, 2 * lanes :])
    sums = jnp.concatenate(sums, axis=0)
    sums = sums.transpose(1, 0, 2).reshape(lanes, width)
    coupling = masked_f * sums[-1][None, :] - sums[:-1]
    return weight[None] * weight[None] * masked_f + weight[None] * coupling


def split_three(values):
    high = lax.reduce_precision(values, exponent_bits=8, mantissa_bits=7)
    rest = values - high
    middle = lax.reduce_precision(rest, exponent_bits=8, mantissa_bits=7)
    low = rest - middle
    return jnp.concatenate([high, middle, low], axis=0).astype(jnp.bfloat16)


def rim_values(values, split, send_lists):
    slots = values.shape[1]
    lanes = values.shape[0]
    index = send_lists[0].reshape(1, -1)
    chosen = jnp.arange(slots, dtype=jnp.int32)[:, None] == index
    parts = jnp.dot(split, chosen.astype(jnp.bfloat16), preferred_element_type=jnp.float32)
    picked = parts[:lanes] + parts[lanes : 2 * lanes] + parts[2 * lanes :]
    rim = picked.shape[1] // 2
    padded = padded_2(picked, (("cell", 1),), rim)
    return jnp.concatenate([padded[:, :rim], padded[:, 3 * rim :]], axis=1)


def smooth_chunk(masked_f, weight, send_lists, neighbours, first, chunk):
    slots = masked_f.shape[1]
    values = jnp.concatenate([masked_f * weight[None, :], weight[None, :]], axis=0)
    lanes = values.shape[0]
    split = split_three(values)
    rim_split = split_three(rim_values(values, split, send_lists))
    reach = 64
    extended = jnp.pad(split, ((0, 0), (reach, reach)))
    local = lax.dynamic_slice_in_dim(extended, first, chunk + 2 * reach, axis=1)
    window = jnp.concatenate([local, rim_split], axis=1)
    faces = lax.dynamic_slice_in_dim(neighbours, first, chunk, axis=1)
    span_local = chunk + 2 * reach
    column = jnp.where(
        faces < slots,
        faces - first + reach,
        jnp.where(faces < slots + rim_split.shape[1], span_local + faces - slots, -1),
    )
    target = jnp.arange(window.shape[1], dtype=jnp.int32)[:, None]
    hits = jnp.zeros((window.shape[1], chunk), jnp.float32)
    for k in range(column.shape[0]):
        hits = hits + (column[k][None, :] == target).astype(jnp.float32)
    parts = jnp.dot(window, hits.astype(jnp.bfloat16), preferred_element_type=jnp.float32)
    sums = parts[:lanes] + parts[lanes : 2 * lanes] + parts[2 * lanes :]
    own_p = lax.dynamic_slice_in_dim(masked_f, first, chunk, axis=1)
    own_w = lax.dynamic_slice_in_dim(weight, first, chunk, axis=0)
    coupling = own_p * sums[-1][None, :] - sums[:-1]
    return own_w[None] * own_w[None] * own_p + own_w[None] * coupling


def on_device(sensitivity, direction, depth_weight, counts, send_lists, neighbours):
    slots = sensitivity.shape[1]
    nvecs = direction.shape[0]
    live = jnp.arange(slots, dtype=jnp.int32) < counts[0]
    masked = jnp.where(live[None, :], direction, jnp.zeros_like(direction))
    partial_data = lax.dot_general(
        masked, sensitivity, (((1,), (1,)), ((), ())), preferred_element_type=jnp.float32
    )
    summed, _ = butterfly_sum(partial_data, "cell")
    rounded = summed.astype(jnp.bfloat16)
    remainder = (summed - rounded.astype(jnp.float32)).astype(jnp.bfloat16)
    stacked = jnp.concatenate([rounded, remainder], axis=0)
    both = jnp.dot(stacked, sensitivity, preferred_element_type=jnp.float32)
    partial_cells = both[:nvecs] + both[nvecs:]
    count = lax.axis_size("dp")
    chunk = slots // count
    me = lax.axis_index("dp")
    first = me * chunk
    pieces = partial_cells.reshape(nvecs, count, chunk).transpose(1, 0, 2)
    pieces = lax.all_to_all(pieces, "dp", 0, 0)
    misfit = pieces[0]
    for source in range(1, count):
        misfit = misfit + pieces[source]
    weight = jnp.where(live, depth_weight, jnp.float32(0.0))
    masked_f = masked.astype(jnp.float32)
    smooth = smooth_chunk(masked_f, weight, send_lists, neighbours, first, chunk)
    total = misfit + 0.5 * smooth
    live_chunk = lax.dynamic_slice_in_dim(live, first, chunk, axis=0)
    product = jnp.where(live_chunk[None, :], total, jnp.float32(0.0))
    return lax.all_gather(product, "dp", axis=1, tiled=True)


def solution(mesh):
    placed = (
        P("dp", "cell"),
        P(None, "cell"),
        P("cell"),
        P("cell"),
        P("cell", None, None),
        P(None, "cell"),
    )
    step = jax.shard_map(
        on_device, mesh=mesh, in_specs=placed, out_specs=P(None, "cell"), check_vma=False
    )
    return step
```

profile of v0, /device:TPU:1, one launch (start us, length us, event | category | flops | bytes accessed | tf_op | source)
XLA Modules:
  0.0 96.7 jit_solution(378828100598284478)
XLA Ops:
  0.0 0.0 copy-start
  0.8 0.8 broadcast_select_fusion.2
  1.6 1.0 %broadcast_multiply_fusion = f32[16,6272]{1,0:T(8,128)S(1)} fusion(f32[6272]{0:T(1024)S(1)} %broadcast_select_fusion.2, bf16[16,6272]{1,0:T(8,128)(2,1)} %param.7, pred[6272]{0:T(1024)(128)(4,1)S(1)} %iota_compare_fusion.8), kind=kLoop, calls=%fused_computation.21 | loop fusion | flops 301056 | bytes 633472 | tf_op jit(solution)/shard_map/mul | solution.py:172
  2.6 0.0 copy-start.2
  2.6 0.1 reduce-precision_convert_fusion.1
  2.7 0.2 pad_maximum_fusion
  2.9 0.0 copy-start.1
  2.9 0.3 copy-done.2
  3.2 1.3 %fusion = f32[51,256]{1,0:T(8,128)S(1)} fusion(bf16[51,6272]{1,0:T(8,128)(2,1)S(1)} %pad_maximum_fusion, s32[256]{0:T(256)S(1)} %bitcast.35), kind=kOutput, calls=%fused_computation.1 | convolution fusion | flops 165380096 | bytes 692992 | tf_op jit(solution)/shard_map/dot_general | solution.py:163
  4.6 4.8 %collective-permute-start.5 = (f32[17,128]{1,0:T(8,128)S(1)}, f32[17,128]{1,0:T(8,128)S(1)}, u32[]{:S(2)}, u32[]{:S(2)}) collective-permute-start(f32[17,128]{1,0:T(8,128)S(1)} %get-tuple-element.14), channel_id=1, source_target_pairs={{0,1},{1,2},{2,3},{3,4},{4,5},{5,6},{6,7},{7,8},{8,9},{9,10},{10,1... | collective-permute-start | bytes 26120 | tf_op jit(solution)/shard_map/ppermute | solution.py:14
  9.4 1.3 %collective-permute-start.6 = (f32[17,128]{1,0:T(8,128)S(1)}, f32[17,128]{1,0:T(8,128)S(1)}, u32[]{:S(2)}, u32[]{:S(2)}) collective-permute-start(f32[17,128]{1,0:T(8,128)S(1)} %get-tuple-element.13), channel_id=1, source_target_pairs={{1,0},{2,1},{3,2},{4,3},{5,4},{6,5},{7,6},{8,7},{9,8},{10,9},{11,1... | collective-permute-start | bytes 26120 | tf_op jit(solution)/shard_map/ppermute | solution.py:15
  10.7 0.0 copy-done
  10.7 0.0 copy-done.1
  10.7 0.5 fusion.5
  11.2 4.7 %collective-permute-start = (f32[16,128]{1,0:T(8,128)S(1)}, f32[16,128]{1,0:T(8,128)S(1)}, u32[]{:S(2)}, u32[]{:S(2)}) collective-permute-start(f32[16,128]{1,0:T(8,128)S(1)} %fusion.5), channel_id=1, source_target_pairs={{0,1},{1,0},{2,3},{3,2},{4,5},{5,4},{6,7},{7,6},{8,9},{9,8},{10,11... | collective-permute-start | bytes 24584 | tf_op jit(solution)/shard_map/ppermute | solution.py:26
  15.9 0.1 fusion.4
  16.0 0.8 select_select_fusion
  16.8 0.1 collective-permute-done
  16.9 7.0 %collective-permute-start.1 = (f32[16,128]{1,0:T(8,128)S(1)}, f32[16,128]{1,0:T(8,128)S(1)}, u32[]{:S(2)}, u32[]{:S(2)}) collective-permute-start(f32[16,128]{1,0:T(8,128)S(1)} %add.125), channel_id=1, source_target_pairs={{0,2},{1,3},{2,0},{3,1},{4,6},{5,7},{6,4},{7,5},{8,10},{9,11},{10,... | collective-permute-start | bytes 24584 | tf_op jit(solution)/shard_map/ppermute | solution.py:26
  24.0 1.0 %collective-permute-done.1 = f32[16,128]{1,0:T(8,128)S(1)} collective-permute-done((f32[16,128]{1,0:T(8,128)S(1)}, f32[16,128]{1,0:T(8,128)S(1)}, u32[]{:S(2)}, u32[]{:S(2)}) %collective-permute-start.1) | collective-permute-done | bytes 8224 | tf_op jit(solution)/shard_map/ppermute | solution.py:26
  25.0 7.8 %collective-permute-start.2 = (f32[16,128]{1,0:T(8,128)S(1)}, f32[16,128]{1,0:T(8,128)S(1)}, u32[]{:S(2)}, u32[]{:S(2)}) collective-permute-start(f32[16,128]{1,0:T(8,128)S(1)} %add.126), channel_id=1, source_target_pairs={{0,4},{1,5},{2,6},{3,7},{4,0},{5,1},{6,2},{7,3},{8,12},{9,13},{10,... | collective-permute-start | bytes 24584 | tf_op jit(solution)/shard_map/ppermute | solution.py:26
  32.8 0.1 pad_dynamic-slice_fusion
  32.9 0.9 collective-permute-done.2
  33.8 5.8 %collective-permute-start.3 = (f32[16,128]{1,0:T(8,128)S(1)}, f32[16,128]{1,0:T(8,128)S(1)}, u32[]{:S(2)}, u32[]{:S(2)}) collective-permute-start(f32[16,128]{1,0:T(8,128)S(1)} %add.127), channel_id=1, source_target_pairs={{0,8},{1,9},{2,10},{3,11},{4,12},{5,13},{6,14},{7,15},{8,0},{9,1},... | collective-permute-start | bytes 24584 | tf_op jit(solution)/shard_map/ppermute | solution.py:26
  39.6 0.1 fusion.29
  39.7 0.1 dynamic_slice.15
  39.8 0.9 collective-permute-done.3
  40.7 4.9 %collective-permute-start.4 = (f32[16,128]{1,0:T(8,128)S(1)}, f32[16,128]{1,0:T(8,128)S(1)}, u32[]{:S(2)}, u32[]{:S(2)}) collective-permute-start(f32[16,128]{1,0:T(8,128)S(1)} %add.128), channel_id=1, source_target_pairs={{0,16},{1,17},{2,18},{3,19},{4,20},{5,21},{6,22},{7,23},{8,24},{9,... | collective-permute-start | bytes 24584 | tf_op jit(solution)/shard_map/ppermute | solution.py:26
  45.6 0.0 collective-permute-done.5
  45.6 1.0 %collective-permute-done.4 = f32[16,128]{1,0:T(8,128)S(1)} collective-permute-done((f32[16,128]{1,0:T(8,128)S(1)}, f32[16,128]{1,0:T(8,128)S(1)}, u32[]{:S(2)}, u32[]{:S(2)}) %collective-permute-start.4) | collective-permute-done | bytes 8224 | tf_op jit(solution)/shard_map/ppermute | solution.py:26
  46.6 0.3 fusion.22
  47.0 0.5 reshape.17
  47.5 1.1 %copy.13 = f32[16,16,392]{2,0,1:T(8,128)} copy(f32[16,16,392]{2,1,0:T(8,128)S(1)} %reshape.17) | data formatting | bytes 802816 | tf_op jit(solution)/shard_map/reshape | solution.py:217
  48.6 13.5 %all-to-all-start = ((f32[16,16,392]{2,1,0:T(8,128)}), f32[16,16,392]{2,1,0:T(8,128)S(1)}, u32[]{:S(2)}, u32[]{:S(2)}) async-start(f32[16,16,392]{2,1,0:T(8,128)} %bitcast.25), calls=%async_computation | async-start | bytes 1048576 | tf_op jit(solution)/shard_map/all_to_all | solution.py:218
  62.2 0.0 collective-permute-done.6
  62.2 1.1 %fusion.2 = f32[51,392]{1,0:T(8,128)S(1)} fusion(s32[392]{0:T(512)S(1)} %bitcast.30, s32[392]{0:T(512)S(1)} %bitcast.31, s32[392]{0:T(512)S(1)} %bitcast.32, s32[392]{0:T(512)S(1)} %bitcast.33, s32[392]{0:T(512)S(1)} %bitcast.34, s32[392]{0:T(512)S(1)} %bitcast.29, bf16[17,256]{1,0:T(8,128)(2,1)S(1)} %get-tuple-element.11, ...), kind=kOutput, calls=%fused_computation.14 | convolution fusion | flops 36819648 | bytes 168528 | tf_op jit(solution)/shard_map/dot_general | solution.py:191
  63.3 16.0 %all-to-all-done = f32[16,16,392]{2,1,0:T(8,128)S(1)} async-done(((f32[16,16,392]{2,1,0:T(8,128)}), f32[16,16,392]{2,1,0:T(8,128)S(1)}, u32[]{:S(2)}, u32[]{:S(2)}) %all-to-all-start) | async-done | bytes 401440 | tf_op jit(solution)/shard_map/all_to_all | solution.py:218
  79.4 0.1 fusion.19
  79.5 15.9 %all-gather = f32[16,392,16]{1,2,0:T(8,128)S(1)} all-gather(f32[1,392,16]{1,2,0:T(8,128)S(1)} %fusion.19), channel_id=1, replica_groups=mesh['dp'=16,'cell'=32] {'dp'}, dimensions={0}, use_global_device_ids=true | all-gather | bytes 426496 | tf_op jit(solution)/shard_map/all_gather | solution.py:228
  95.4 0.3 copy.11
  95.7 1.0 %reshape.27 = f32[6272,16]{0,1:T(8,128)} reshape(f32[16,392,16]{1,0,2:T(8,128)S(1)} %copy.11) | data formatting | bytes 802816
  (16 shorter events, 0.1 us)
Async XLA Ops:
  0.0 10.7 %copy-start = (bf16[128,6272]{1,0:T(8,128)(2,1)S(1)}, bf16[128,6272]{1,0:T(8,128)(2,1)}, u32[]{:S(2)}) copy-start(bf16[128,6272]{1,0:T(8,128)(2,1)} %param.6) | copy-start | bytes 4816900
  2.6 0.7 copy-start.2
  2.9 7.8 %copy-start.1 = (bf16[16,6272]{1,0:T(8,128)(2,1)S(1)}, bf16[16,6272]{1,0:T(8,128)(2,1)}, u32[]{:S(2)}) copy-start(bf16[16,6272]{1,0:T(8,128)(2,1)} %param.7) | copy-start | bytes 602116
  4.6 41.0 %collective-permute-start.5 = (f32[17,128]{1,0:T(8,128)S(1)}, f32[17,128]{1,0:T(8,128)S(1)}, u32[]{:S(2)}, u32[]{:S(2)}) collective-permute-start(f32[17,128]{1,0:T(8,128)S(1)} %get-tuple-element.14), channel_id=1, source_target_pairs={{0,1},{1,2},{2,3},{3,4},{4,5},{5,6},{6,7},{7,8},{8,9},{9,10},{10,1... | collective-permute-start | bytes 26120 | tf_op jit(solution)/shard_map/ppermute | solution.py:14
  9.4 52.7 %collective-permute-start.6 = (f32[17,128]{1,0:T(8,128)S(1)}, f32[17,128]{1,0:T(8,128)S(1)}, u32[]{:S(2)}, u32[]{:S(2)}) collective-permute-start(f32[17,128]{1,0:T(8,128)S(1)} %get-tuple-element.13), channel_id=1, source_target_pairs={{1,0},{2,1},{3,2},{4,3},{5,4},{6,5},{7,6},{8,7},{9,8},{10,9},{11,1... | collective-permute-start | bytes 26120 | tf_op jit(solution)/shard_map/ppermute | solution.py:15
  11.2 5.7 %collective-permute-start = (f32[16,128]{1,0:T(8,128)S(1)}, f32[16,128]{1,0:T(8,128)S(1)}, u32[]{:S(2)}, u32[]{:S(2)}) collective-permute-start(f32[16,128]{1,0:T(8,128)S(1)} %fusion.5), channel_id=1, source_target_pairs={{0,1},{1,0},{2,3},{3,2},{4,5},{5,4},{6,7},{7,6},{8,9},{9,8},{10,11... | collective-permute-start | bytes 24584 | tf_op jit(solution)/shard_map/ppermute | solution.py:26
  16.9 8.0 %collective-permute-start.1 = (f32[16,128]{1,0:T(8,128)S(1)}, f32[16,128]{1,0:T(8,128)S(1)}, u32[]{:S(2)}, u32[]{:S(2)}) collective-permute-start(f32[16,128]{1,0:T(8,128)S(1)} %add.125), channel_id=1, source_target_pairs={{0,2},{1,3},{2,0},{3,1},{4,6},{5,7},{6,4},{7,5},{8,10},{9,11},{10,... | collective-permute-start | bytes 24584 | tf_op jit(solution)/shard_map/ppermute | solution.py:26
  25.0 8.8 %collective-permute-start.2 = (f32[16,128]{1,0:T(8,128)S(1)}, f32[16,128]{1,0:T(8,128)S(1)}, u32[]{:S(2)}, u32[]{:S(2)}) collective-permute-start(f32[16,128]{1,0:T(8,128)S(1)} %add.126), channel_id=1, source_target_pairs={{0,4},{1,5},{2,6},{3,7},{4,0},{5,1},{6,2},{7,3},{8,12},{9,13},{10,... | collective-permute-start | bytes 24584 | tf_op jit(solution)/shard_map/ppermute | solution.py:26
  33.8 6.8 %collective-permute-start.3 = (f32[16,128]{1,0:T(8,128)S(1)}, f32[16,128]{1,0:T(8,128)S(1)}, u32[]{:S(2)}, u32[]{:S(2)}) collective-permute-start(f32[16,128]{1,0:T(8,128)S(1)} %add.127), channel_id=1, source_target_pairs={{0,8},{1,9},{2,10},{3,11},{4,12},{5,13},{6,14},{7,15},{8,0},{9,1},... | collective-permute-start | bytes 24584 | tf_op jit(solution)/shard_map/ppermute | solution.py:26
  40.7 5.9 %collective-permute-start.4 = (f32[16,128]{1,0:T(8,128)S(1)}, f32[16,128]{1,0:T(8,128)S(1)}, u32[]{:S(2)}, u32[]{:S(2)}) collective-permute-start(f32[16,128]{1,0:T(8,128)S(1)} %add.128), channel_id=1, source_target_pairs={{0,16},{1,17},{2,18},{3,19},{4,20},{5,21},{6,22},{7,23},{8,24},{9,... | collective-permute-start | bytes 24584 | tf_op jit(solution)/shard_map/ppermute | solution.py:26
  48.6 30.7 %all-to-all-start = ((f32[16,16,392]{2,1,0:T(8,128)}), f32[16,16,392]{2,1,0:T(8,128)S(1)}, u32[]{:S(2)}, u32[]{:S(2)}) async-start(f32[16,16,392]{2,1,0:T(8,128)} %bitcast.25), calls=%async_computation | async-start | bytes 1048576 | tf_op jit(solution)/shard_map/all_to_all | solution.py:218
where the time goes:
time: 97.2 us; the launch traced here: 96.7 us
  starting transfers between devices  49.8 us (51%)
  waiting for transfers between devices  20 us (21%)
  blocking collectives  15.9 us (16%)
  local copies, waits for them, and re-layouts  3.53 us (4%)
  matrix products  3.23 us (3%)
  other arithmetic  3.21 us (3%)
  between operations  1.03 us (1%)
    ppermute x5, starting transfers between devices, butterfly_sum(): value = value + lax.ppermute(value, axis, pairs)  30.2 us
    all_to_all x1, waiting for transfers between devices, on_device(): pieces = lax.all_to_all(pieces, 'dp', 0, 0)  16 us
    all_gather x1, blocking collectives, on_device(): return lax.all_gather(product, 'dp', axis=1, tiled=True)  15.9 us
    all_to_all x1, starting transfers between devices, on_device(): pieces = lax.all_to_all(pieces, 'dp', 0, 0)  13.5 us
    ppermute x1, starting transfers between devices, padded_2(): before = lax.ppermute(last, axis, up)  4.82 us
    ppermute x5, waiting for transfers between devices, butterfly_sum(): value = value + lax.ppermute(value, axis, pairs)  3.93 us
  transfers between devices with their start and end apart: 8, of which 6 were waited for; matrix products, arithmetic and copies ran while one was open for 5% of the time, Pallas kernels for 0%

commit v1 on v0

--- a/solution.py
+++ b/solution.py
@@ -1,7 +1,7 @@
 import jax
 import jax.numpy as jnp
 from jax import lax
-from jax.sharding import PartitionSpec as P
+from jax.sharding import Mesh, PartitionSpec as P
 
 
 def padded_2(value, sides, width):
@@ -96,7 +96,7 @@
     chosen_parts = jnp.dot(split, chosen.astype(jnp.bfloat16), preferred_element_type=jnp.float32)
     picked = chosen_parts[:lanes] + chosen_parts[lanes : 2 * lanes] + chosen_parts[2 * lanes :]
     rim = picked.shape[1] // 2
-    padded = padded_2(picked, (("cell", 1),), rim)
+    padded = padded_2(picked, ((CELL, 1),), rim)
     rim_vals = jnp.concatenate([padded[:, :rim], padded[:, 3 * rim :]], axis=1)
     rim_high = lax.reduce_precision(rim_vals, exponent_bits=8, mantissa_bits=7)
     rim_rest = rim_vals - rim_high
@@ -163,7 +163,7 @@
     parts = jnp.dot(split, chosen.astype(jnp.bfloat16), preferred_element_type=jnp.float32)
     picked = parts[:lanes] + parts[lanes : 2 * lanes] + parts[2 * lanes :]
     rim = picked.shape[1] // 2
-    padded = padded_2(picked, (("cell", 1),), rim)
+    padded = padded_2(picked, ((CELL, 1),), rim)
     return jnp.concatenate([padded[:, :rim], padded[:, 3 * rim :]], axis=1)
 
 
@@ -204,18 +204,18 @@
     partial_data = lax.dot_general(
         masked, sensitivity, (((1,), (1,)), ((), ())), preferred_element_type=jnp.float32
     )
-    summed, _ = butterfly_sum(partial_data, "cell")
+    summed = lax.psum(lax.psum(partial_data, "z"), "x")
     rounded = summed.astype(jnp.bfloat16)
     remainder = (summed - rounded.astype(jnp.float32)).astype(jnp.bfloat16)
     stacked = jnp.concatenate([rounded, remainder], axis=0)
     both = jnp.dot(stacked, sensitivity, preferred_element_type=jnp.float32)
     partial_cells = both[:nvecs] + both[nvecs:]
-    count = lax.axis_size("dp")
+    count = lax.axis_size(DP)
     chunk = slots // count
-    me = lax.axis_index("dp")
+    me = lax.axis_index(DP)
     first = me * chunk
     pieces = partial_cells.reshape(nvecs, count, chunk).transpose(1, 0, 2)
-    pieces = lax.all_to_all(pieces, "dp", 0, 0)
+    pieces = lax.all_to_all(pieces, DP, 0, 0)
     misfit = pieces[0]
     for source in range(1, count):
         misfit = misfit + pieces[source]
@@ -225,19 +225,28 @@
     total = misfit + 0.5 * smooth
     live_chunk = lax.dynamic_slice_in_dim(live, first, chunk, axis=0)
     product = jnp.where(live_chunk[None, :], total, jnp.float32(0.0))
-    return lax.all_gather(product, "dp", axis=1, tiled=True)
+    return lax.all_gather(product, DP, axis=1, tiled=True)
+
+
+DP = ("y", "core")
+CELL = ("x", "z")
 
 
 def solution(mesh):
+    dp_size, cell_size = mesh.devices.shape
+    z_size = 8 if cell_size % 8 == 0 else cell_size
+    split_mesh = Mesh(
+        mesh.devices.reshape(dp_size // 2, 2, cell_size // z_size, z_size), DP + CELL
+    )
     placed = (
-        P("dp", "cell"),
-        P(None, "cell"),
-        P("cell"),
-        P("cell"),
-        P("cell", None, None),
-        P(None, "cell"),
+        P(DP, CELL),
+        P(None, CELL),
+        P(CELL),
+        P(CELL),
+        P(CELL, None, None),
+        P(None, CELL),
     )
     step = jax.shard_map(
-        on_device, mesh=mesh, in_specs=placed, out_specs=P(None, "cell"), check_vma=False
+        on_device, mesh=split_mesh, in_specs=placed, out_specs=P(None, CELL), check_vma=False
     )
     return step

time: 97.2 us -> 90.7 us (0.933)
  starting transfers between devices: 49.8 us -> 19.9 us
  blocking collectives: 15.9 us -> 44.5 us
  waiting for transfers between devices: 20 us -> 14.9 us
    ppermute x5 -> x0, starting transfers between devices: 30.2 us -> none  [butterfly_sum(): value = value + lax.ppermute(value, axis, pairs)]
    psum x0 -> x2, blocking collectives: none -> 28.6 us  [on_device(): summed = lax.psum(lax.psum(partial_data, 'z'), 'x')]
    ppermute x5 -> x0, waiting for transfers between devices: 3.93 us -> none  [butterfly_sum(): value = value + lax.ppermute(value, axis, pairs)]
    all_to_all x1, waiting for transfers between devices: 16 us -> 14.9 us  [on_device(): pieces = lax.all_to_all(pieces, DP, 0, 0)]
  transfers between devices with their start and end apart: 8 -> 3, of which waited for: 6 -> 1; matrix products, arithmetic and copies ran while one was open for 5% -> 5% of each run, Pallas kernels for 0% -> 0%
where the time goes in v1:
time: 90.7 us; the launch traced here: 90.3 us
  blocking collectives  44.5 us (49%)
  starting transfers between devices  19.9 us (22%)
  waiting for transfers between devices  14.9 us (16%)
  local copies, waits for them, and re-layouts  3.52 us (4%)
  matrix products  3.23 us (4%)
  other arithmetic  3.2 us (4%)
  between operations  0.98 us (1%)
    psum x2, blocking collectives, on_device(): summed = lax.psum(lax.psum(partial_data, 'z'), 'x')  28.6 us
    all_gather x1, blocking collectives, on_device(): return lax.all_gather(product, DP, axis=1, tiled=True)  15.9 us
    all_to_all x1, waiting for transfers between devices, on_device(): pieces = lax.all_to_all(pieces, DP, 0, 0)  14.9 us
    all_to_all x1, starting transfers between devices, on_device(): pieces = lax.all_to_all(pieces, DP, 0, 0)  13.8 us
    ppermute x1, starting transfers between devices, padded_2(): before = lax.ppermute(last, axis, up)  4.81 us
  transfers between devices with their start and end apart: 3, of which 1 were waited for; matrix products, arithmetic and copies ran while one was open for 5% of the time, Pallas kernels for 0%

profile of v1, /device:TPU:1, one launch (start us, length us, event | category | flops | bytes accessed | tf_op | source)
XLA Modules:
  0.0 90.3 jit_solution(2275734415088678889)
XLA Ops:
  0.0 0.0 copy-start
  0.8 0.8 broadcast_select_fusion.2
  1.6 1.0 %broadcast_multiply_fusion = f32[16,6272]{1,0:T(8,128)S(1)} fusion(f32[6272]{0:T(1024)S(1)} %broadcast_select_fusion.2, bf16[16,6272]{1,0:T(8,128)(2,1)} %param.7, pred[6272]{0:T(1024)(128)(4,1)S(1)} %iota_compare_fusion.8), kind=kLoop, calls=%fused_computation.21 | loop fusion | flops 301056 | bytes 633472 | tf_op jit(solution)/shard_map/mul | solution.py:172
  2.6 0.0 copy-start.2
  2.6 0.1 reduce-precision_convert_fusion.1
  2.7 0.2 pad_maximum_fusion
  2.9 0.0 copy-start.1
  2.9 0.3 copy-done.2
  3.2 1.3 %fusion = f32[51,256]{1,0:T(8,128)S(1)} fusion(bf16[51,6272]{1,0:T(8,128)(2,1)S(1)} %pad_maximum_fusion, s32[256]{0:T(256)S(1)} %bitcast.35), kind=kOutput, calls=%fused_computation.1 | convolution fusion | flops 165380096 | bytes 692992 | tf_op jit(solution)/shard_map/dot_general | solution.py:163
  4.6 4.8 %collective-permute-start = (f32[17,128]{1,0:T(8,128)S(1)}, f32[17,128]{1,0:T(8,128)S(1)}, u32[]{:S(2)}, u32[]{:S(2)}) collective-permute-start(f32[17,128]{1,0:T(8,128)S(1)} %get-tuple-element.16), channel_id=1, source_target_pairs={{0,1},{1,2},{2,3},{3,4},{4,5},{5,6},{6,7},{7,8},{8,9},{9,10},{10,1... | collective-permute-start | bytes 26120 | tf_op jit(solution)/shard_map/ppermute | solution.py:14
  9.4 1.3 %collective-permute-start.1 = (f32[17,128]{1,0:T(8,128)S(1)}, f32[17,128]{1,0:T(8,128)S(1)}, u32[]{:S(2)}, u32[]{:S(2)}) collective-permute-start(f32[17,128]{1,0:T(8,128)S(1)} %get-tuple-element.15), channel_id=1, source_target_pairs={{1,0},{2,1},{3,2},{4,3},{5,4},{6,5},{7,6},{8,7},{9,8},{10,9},{11,1... | collective-permute-start | bytes 26120 | tf_op jit(solution)/shard_map/ppermute | solution.py:15
  10.7 0.0 copy-done
  10.7 0.0 copy-done.1
  10.7 0.5 fusion.5
  11.2 20.1 %psum.14 = f32[16,128]{1,0:T(8,128)S(1)} all-reduce(f32[16,128]{1,0:T(8,128)S(1)} %fusion.5), channel_id=1, replica_groups=mesh['y'=8,'core'=2,'x'=4,'z'=8] {'z'}, use_global_device_ids=true, to_apply=%region_0.1 | all-reduce | flops 2048 | bytes 16384 | tf_op jit(solution)/shard_map/psum | solution.py:207
  31.3 8.5 %psum.15 = f32[16,128]{1,0:T(8,128)S(1)} all-reduce(f32[16,128]{1,0:T(8,128)S(1)} %psum.14), channel_id=1, replica_groups=mesh['y'=8,'core'=2,'x'=4,'z'=8] {'x'}, use_global_device_ids=true, to_apply=%region_1.2 | all-reduce | flops 2048 | bytes 16384 | tf_op jit(solution)/shard_map/psum | solution.py:207
  39.9 0.3 fusion.22
  40.3 0.5 reshape.17
  40.8 1.1 %copy.13 = f32[16,16,392]{2,0,1:T(8,128)} copy(f32[16,16,392]{2,1,0:T(8,128)S(1)} %reshape.17) | data formatting | bytes 802816 | tf_op jit(solution)/shard_map/reshape | solution.py:217
  41.9 13.8 %all-to-all-start = ((f32[16,16,392]{2,1,0:T(8,128)}), f32[16,16,392]{2,1,0:T(8,128)S(1)}, u32[]{:S(2)}, u32[]{:S(2)}) async-start(f32[16,16,392]{2,1,0:T(8,128)} %bitcast.25), calls=%async_computation | async-start | bytes 1048576 | tf_op jit(solution)/shard_map/all_to_all | solution.py:218
  55.7 0.1 fusion.4
  55.8 0.1 pad_dynamic-slice_fusion
  55.9 0.8 select_select_fusion
  56.7 0.1 fusion.29
  56.8 0.1 dynamic_slice.15
  56.9 0.0 collective-permute-done
  56.9 0.0 collective-permute-done.1
  56.9 1.1 %fusion.2 = f32[51,392]{1,0:T(8,128)S(1)} fusion(s32[392]{0:T(512)S(1)} %bitcast.30, s32[392]{0:T(512)S(1)} %bitcast.31, s32[392]{0:T(512)S(1)} %bitcast.32, s32[392]{0:T(512)S(1)} %bitcast.33, s32[392]{0:T(512)S(1)} %bitcast.34, s32[392]{0:T(512)S(1)} %bitcast.29, bf16[17,256]{1,0:T(8,128)(2,1)S(1)} %get-tuple-element.13, ...), kind=kOutput, calls=%fused_computation.14 | convolution fusion | flops 36819648 | bytes 168528 | tf_op jit(solution)/shard_map/dot_general | solution.py:191
  58.1 14.9 %all-to-all-done = f32[16,16,392]{2,1,0:T(8,128)S(1)} async-done(((f32[16,16,392]{2,1,0:T(8,128)}), f32[16,16,392]{2,1,0:T(8,128)S(1)}, u32[]{:S(2)}, u32[]{:S(2)}) %all-to-all-start) | async-done | bytes 401440 | tf_op jit(solution)/shard_map/all_to_all | solution.py:218
  72.9 0.1 fusion.19
  73.0 15.9 %all-gather = f32[16,392,16]{1,2,0:T(8,128)S(1)} all-gather(f32[1,392,16]{1,2,0:T(8,128)S(1)} %fusion.19), channel_id=1, replica_groups=mesh['y'=8,'core'=2,'x'=4,'z'=8] {'y','core'}, dimensions={0}, use_global_device_ids=true | all-gather | bytes 426496 | tf_op jit(solution)/shard_map/all_gather | solution.py:228
  88.9 0.3 copy.11
  89.2 1.0 %reshape.27 = f32[6272,16]{0,1:T(8,128)} reshape(f32[16,392,16]{1,0,2:T(8,128)S(1)} %copy.11) | data formatting | bytes 802816
  (12 shorter events, 0.1 us)
Async XLA Ops:
  0.0 10.7 %copy-start = (bf16[128,6272]{1,0:T(8,128)(2,1)S(1)}, bf16[128,6272]{1,0:T(8,128)(2,1)}, u32[]{:S(2)}) copy-start(bf16[128,6272]{1,0:T(8,128)(2,1)} %param.6) | copy-start | bytes 4816900
  2.6 0.7 copy-start.2
  2.9 7.8 %copy-start.1 = (bf16[16,6272]{1,0:T(8,128)(2,1)S(1)}, bf16[16,6272]{1,0:T(8,128)(2,1)}, u32[]{:S(2)}) copy-start(bf16[16,6272]{1,0:T(8,128)(2,1)} %param.7) | copy-start | bytes 602116
  4.6 52.3 %collective-permute-start = (f32[17,128]{1,0:T(8,128)S(1)}, f32[17,128]{1,0:T(8,128)S(1)}, u32[]{:S(2)}, u32[]{:S(2)}) collective-permute-start(f32[17,128]{1,0:T(8,128)S(1)} %get-tuple-element.16), channel_id=1, source_target_pairs={{0,1},{1,2},{2,3},{3,4},{4,5},{5,6},{6,7},{7,8},{8,9},{9,10},{10,1... | collective-permute-start | bytes 26120 | tf_op jit(solution)/shard_map/ppermute | solution.py:14
  9.4 47.5 %collective-permute-start.1 = (f32[17,128]{1,0:T(8,128)S(1)}, f32[17,128]{1,0:T(8,128)S(1)}, u32[]{:S(2)}, u32[]{:S(2)}) collective-permute-start(f32[17,128]{1,0:T(8,128)S(1)} %get-tuple-element.15), channel_id=1, source_target_pairs={{1,0},{2,1},{3,2},{4,3},{5,4},{6,5},{7,6},{8,7},{9,8},{10,9},{11,1... | collective-permute-start | bytes 26120 | tf_op jit(solution)/shard_map/ppermute | solution.py:15
  41.9 31.0 %all-to-all-start = ((f32[16,16,392]{2,1,0:T(8,128)}), f32[16,16,392]{2,1,0:T(8,128)S(1)}, u32[]{:S(2)}, u32[]{:S(2)}) async-start(f32[16,16,392]{2,1,0:T(8,128)} %bitcast.25), calls=%async_computation | async-start | bytes 1048576 | tf_op jit(solution)/shard_map/all_to_all | solution.py:218

commit v2 on v1

v2 whole, which is shorter than its diff:
```python
import jax
import jax.numpy as jnp
from jax import lax
from jax.sharding import Mesh, PartitionSpec as P


def padded_2(value, sides, width):
    for axis, dim in sides:
        count, length = (lax.axis_size(axis), value.shape[dim])
        up = [(i, (i + 1) % count) for i in range(count - 1)]
        down = [(j, i) for i, j in up]
        last = lax.slice_in_dim(value, length - width, length, axis=dim)
        leading = lax.slice_in_dim(value, 0, width, axis=dim)
        before = lax.ppermute(last, axis, up)
        after = lax.ppermute(leading, axis, down)
        value = jnp.concatenate([before, value, after], axis=dim)
    return value


def split_three(values):
    high = lax.reduce_precision(values, exponent_bits=8, mantissa_bits=7)
    rest = values - high
    middle = lax.reduce_precision(rest, exponent_bits=8, mantissa_bits=7)
    low = rest - middle
    return jnp.concatenate([high, middle, low], axis=0).astype(jnp.bfloat16)


def rim_values(values, split, send_lists):
    slots = values.shape[1]
    lanes = values.shape[0]
    index = send_lists[0].reshape(1, -1)
    chosen = jnp.arange(slots, dtype=jnp.int32)[:, None] == index
    parts = jnp.dot(split, chosen.astype(jnp.bfloat16), preferred_element_type=jnp.float32)
    picked = parts[:lanes] + parts[lanes : 2 * lanes] + parts[2 * lanes :]
    rim = picked.shape[1] // 2
    padded = padded_2(picked, ((CELL, 1),), rim)
    return jnp.concatenate([padded[:, :rim], padded[:, 3 * rim :]], axis=1)


def smooth_chunk(masked_f, weight, send_lists, neighbours, first, chunk):
    slots = masked_f.shape[1]
    values = jnp.concatenate([masked_f * weight[None, :], weight[None, :]], axis=0)
    lanes = values.shape[0]
    split = split_three(values)
    rim_split = split_three(rim_values(values, split, send_lists))
    reach = 64
    extended = jnp.pad(split, ((0, 0), (reach, reach)))
    local = lax.dynamic_slice_in_dim(extended, first, chunk + 2 * reach, axis=1)
    window = jnp.concatenate([local, rim_split], axis=1)
    faces = lax.dynamic_slice_in_dim(neighbours, first, chunk, axis=1)
    span_local = chunk + 2 * reach
    column = jnp.where(
        faces < slots,
        faces - first + reach,
        jnp.where(faces < slots + rim_split.shape[1], span_local + faces - slots, -1),
    )
    target = jnp.arange(window.shape[1], dtype=jnp.int32)[:, None]
    hits = jnp.zeros((window.shape[1], chunk), jnp.float32)
    for k in range(column.shape[0]):
        hits = hits + (column[k][None, :] == target).astype(jnp.float32)
    parts = jnp.dot(window, hits.astype(jnp.bfloat16), preferred_element_type=jnp.float32)
    sums = parts[:lanes] + parts[lanes : 2 * lanes] + parts[2 * lanes :]
    own_p = lax.dynamic_slice_in_dim(masked_f, first, chunk, axis=1)
    own_w = lax.dynamic_slice_in_dim(weight, first, chunk, axis=0)
    coupling = own_p * sums[-1][None, :] - sums[:-1]
    return own_w[None] * own_w[None] * own_p + own_w[None] * coupling


def on_device_body(sensitivity, direction, depth_weight, counts, send_lists, neighbours):
    slots = sensitivity.shape[1]
    nvecs = direction.shape[0]
    live = jnp.arange(slots, dtype=jnp.int32) < counts[0]
    masked = jnp.where(live[None, :], direction, jnp.zeros_like(direction))
    partial_data = lax.dot_general(
        masked, sensitivity, (((1,), (1,)), ((), ())), preferred_element_type=jnp.float32
    )
    summed = lax.psum(lax.psum(partial_data, "z"), "x")
    rounded = summed.astype(jnp.bfloat16)
    remainder = (summed - rounded.astype(jnp.float32)).astype(jnp.bfloat16)
    stacked = jnp.concatenate([rounded, remainder], axis=0)
    both = jnp.dot(stacked, sensitivity, preferred_element_type=jnp.float32)
    partial_cells = both[:nvecs] + both[nvecs:]
    count = lax.axis_size(DP)
    chunk = slots // count
    me = lax.axis_index(DP)
    first = me * chunk
    pieces = partial_cells.reshape(nvecs, count, chunk).transpose(1, 0, 2)
    pieces = lax.all_to_all(pieces, DP, 0, 0)
    misfit = pieces[0]
    for source in range(1, count):
        misfit = misfit + pieces[source]
    weight = jnp.where(live, depth_weight, jnp.float32(0.0))
    masked_f = masked.astype(jnp.float32)
    smooth = smooth_chunk(masked_f, weight, send_lists, neighbours, first, chunk)
    total = misfit + 0.5 * smooth
    live_chunk = lax.dynamic_slice_in_dim(live, first, chunk, axis=0)
    product = jnp.where(live_chunk[None, :], total, jnp.float32(0.0))
    gathered = lax.all_gather(product, DP, axis=0)
    return gathered.transpose(1, 0, 2).reshape(nvecs, slots)


DP = ("y", "core")
CELL = ("x", "z")


def solution(mesh):
    dp_size, cell_size = mesh.devices.shape
    z_size = 8 if cell_size % 8 == 0 else cell_size
    split_mesh = Mesh(
        mesh.devices.reshape(dp_size // 2, 2, cell_size // z_size, z_size), DP + CELL
    )
    placed = (
        P(DP, CELL),
        P(None, CELL),
        P(CELL),
        P(CELL),
        P(CELL, None, None),
        P(None, CELL),
    )
    return jax.shard_map(
        on_device_body, mesh=split_mesh, in_specs=placed, out_specs=P(None, CELL), check_vma=False
    )
```

time: 90.7 us -> 90.7 us (level)
    reshape x2 -> x3, local copies, waits for them, and re-layouts: 1.61 us -> 2.65 us  [the longest x2 1.61 us: on_device_body(): pieces = partial_cells.reshape(nvecs, count, chunk).transpose(1, 0, 2)]
    unnamed x8 -> x7, local copies, waits for them, and re-layouts: 1.39 us -> 0.34 us
where the time goes in v2:
time: 90.7 us; the launch traced here: 90.3 us
  blocking collectives  44.5 us (49%)
  starting transfers between devices  19.9 us (22%)
  waiting for transfers between devices  14.9 us (16%)
  local copies, waits for them, and re-layouts  3.52 us (4%)
  matrix products  3.23 us (4%)
  other arithmetic  3.2 us (4%)
  between operations  0.98 us (1%)
    psum x2, blocking collectives, on_device_body(): summed = lax.psum(lax.psum(partial_data, 'z'), 'x')  28.6 us
    all_gather x1, blocking collectives, on_device_body(): gathered = lax.all_gather(product, DP, axis=0)  15.9 us
    all_to_all x1, waiting for transfers between devices, on_device_body(): pieces = lax.all_to_all(pieces, DP, 0, 0)  14.9 us
    all_to_all x1, starting transfers between devices, on_device_body(): pieces = lax.all_to_all(pieces, DP, 0, 0)  13.8 us
    ppermute x1, starting transfers between devices, padded_2(): before = lax.ppermute(last, axis, up)  4.81 us
  transfers between devices with their start and end apart: 3, of which 1 were waited for; matrix products, arithmetic and copies ran while one was open for 5% of the time, Pallas kernels for 0%

profile of v2, /device:TPU:1, one launch (start us, length us, event | category | flops | bytes accessed | tf_op | source)
XLA Modules:
  0.0 90.3 jit_solution(11925614409582386226)
XLA Ops:
  0.0 0.0 copy-start
  0.8 0.8 broadcast_select_fusion.2
  1.6 1.0 %broadcast_multiply_fusion = f32[16,6272]{1,0:T(8,128)S(1)} fusion(f32[6272]{0:T(1024)S(1)} %broadcast_select_fusion.2, bf16[16,6272]{1,0:T(8,128)(2,1)} %param.7, pred[6272]{0:T(1024)(128)(4,1)S(1)} %iota_compare_fusion.8), kind=kLoop, calls=%fused_computation.21 | loop fusion | flops 301056 | bytes 633472 | tf_op jit(solution)/shard_map/mul | solution.py:42
  2.6 0.0 copy-start.2
  2.6 0.1 reduce-precision_convert_fusion.1
  2.7 0.2 pad_maximum_fusion
  2.9 0.0 copy-start.1
  2.9 0.3 copy-done.2
  3.2 1.3 %fusion = f32[51,256]{1,0:T(8,128)S(1)} fusion(bf16[51,6272]{1,0:T(8,128)(2,1)S(1)} %pad_maximum_fusion, s32[256]{0:T(256)S(1)} %bitcast.32), kind=kOutput, calls=%fused_computation.1 | convolution fusion | flops 165380096 | bytes 692992 | tf_op jit(solution)/shard_map/dot_general | solution.py:33
  4.6 4.8 %collective-permute-start = (f32[17,128]{1,0:T(8,128)S(1)}, f32[17,128]{1,0:T(8,128)S(1)}, u32[]{:S(2)}, u32[]{:S(2)}) collective-permute-start(f32[17,128]{1,0:T(8,128)S(1)} %get-tuple-element.16), channel_id=1, source_target_pairs={{0,1},{1,2},{2,3},{3,4},{4,5},{5,6},{6,7},{7,8},{8,9},{9,10},{10,1... | collective-permute-start | bytes 26120 | tf_op jit(solution)/shard_map/ppermute | solution.py:14
  9.4 1.3 %collective-permute-start.1 = (f32[17,128]{1,0:T(8,128)S(1)}, f32[17,128]{1,0:T(8,128)S(1)}, u32[]{:S(2)}, u32[]{:S(2)}) collective-permute-start(f32[17,128]{1,0:T(8,128)S(1)} %get-tuple-element.15), channel_id=1, source_target_pairs={{1,0},{2,1},{3,2},{4,3},{5,4},{6,5},{7,6},{8,7},{9,8},{10,9},{11,1... | collective-permute-start | bytes 26120 | tf_op jit(solution)/shard_map/ppermute | solution.py:15
  10.7 0.0 copy-done
  10.7 0.0 copy-done.1
  10.7 0.5 fusion.5
  11.2 20.1 %psum.14 = f32[16,128]{1,0:T(8,128)S(1)} all-reduce(f32[16,128]{1,0:T(8,128)S(1)} %fusion.5), channel_id=1, replica_groups=mesh['y'=8,'core'=2,'x'=4,'z'=8] {'z'}, use_global_device_ids=true, to_apply=%region_0.1 | all-reduce | flops 2048 | bytes 16384 | tf_op jit(solution)/shard_map/psum | solution.py:77
  31.3 8.5 %psum.15 = f32[16,128]{1,0:T(8,128)S(1)} all-reduce(f32[16,128]{1,0:T(8,128)S(1)} %psum.14), channel_id=1, replica_groups=mesh['y'=8,'core'=2,'x'=4,'z'=8] {'x'}, use_global_device_ids=true, to_apply=%region_1.2 | all-reduce | flops 2048 | bytes 16384 | tf_op jit(solution)/shard_map/psum | solution.py:77
  39.9 0.3 fusion.21
  40.3 0.5 reshape.20
  40.8 1.1 %copy.10 = f32[16,16,392]{2,0,1:T(8,128)} copy(f32[16,16,392]{2,1,0:T(8,128)S(1)} %reshape.20) | data formatting | bytes 802816 | tf_op jit(solution)/shard_map/reshape | solution.py:87
  41.9 13.8 %all-to-all-start = ((f32[16,16,392]{2,1,0:T(8,128)}), f32[16,16,392]{2,1,0:T(8,128)S(1)}, u32[]{:S(2)}, u32[]{:S(2)}) async-start(f32[16,16,392]{2,1,0:T(8,128)} %bitcast.21), calls=%async_computation | async-start | bytes 1048576 | tf_op jit(solution)/shard_map/all_to_all | solution.py:88
  55.7 0.1 fusion.4
  55.8 0.1 pad_dynamic-slice_fusion
  55.9 0.8 select_select_fusion
  56.7 0.1 fusion.28
  56.8 0.1 dynamic_slice.15
  56.9 0.0 collective-permute-done
  56.9 0.0 collective-permute-done.1
  56.9 1.1 %fusion.2 = f32[51,392]{1,0:T(8,128)S(1)} fusion(s32[392]{0:T(512)S(1)} %bitcast.27, s32[392]{0:T(512)S(1)} %bitcast.28, s32[392]{0:T(512)S(1)} %bitcast.29, s32[392]{0:T(512)S(1)} %bitcast.30, s32[392]{0:T(512)S(1)} %bitcast.31, s32[392]{0:T(512)S(1)} %bitcast.26, bf16[17,256]{1,0:T(8,128)(2,1)S(1)} %get-tuple-element.13, ...), kind=kOutput, calls=%fused_computation.14 | convolution fusion | flops 36819648 | bytes 168528 | tf_op jit(solution)/shard_map/dot_general | solution.py:61
  58.1 14.9 %all-to-all-done = f32[16,16,392]{2,1,0:T(8,128)S(1)} async-done(((f32[16,16,392]{2,1,0:T(8,128)}), f32[16,16,392]{2,1,0:T(8,128)S(1)}, u32[]{:S(2)}, u32[]{:S(2)}) %all-to-all-start) | async-done | bytes 401440 | tf_op jit(solution)/shard_map/all_to_all | solution.py:88
  72.9 0.1 fusion.18
  73.0 15.9 %all-gather = f32[256,392]{1,0:T(8,128)S(1)} all-gather(f32[16,392]{1,0:T(8,128)S(1)} %fusion.18), channel_id=2, replica_groups=mesh['y'=8,'core'=2,'x'=4,'z'=8] {'y','core'}, dimensions={0}, use_global_device_ids=true | all-gather | bytes 426496 | tf_op jit(solution)/shard_map/all_gather | solution.py:98
  88.9 0.3 copy.8
  89.2 1.0 %reshape.21 = f32[16,6272]{1,0:T(8,128)} reshape(f32[16,16,392]{2,1,0:T(8,128)S(1)} %copy.8) | data formatting | bytes 802816 | tf_op jit(solution)/shard_map/reshape | solution.py:99
  (12 shorter events, 0.1 us)
Async XLA Ops:
  0.0 10.7 %copy-start = (bf16[128,6272]{1,0:T(8,128)(2,1)S(1)}, bf16[128,6272]{1,0:T(8,128)(2,1)}, u32[]{:S(2)}) copy-start(bf16[128,6272]{1,0:T(8,128)(2,1)} %param.6) | copy-start | bytes 4816900
  2.6 0.7 copy-start.2
  2.9 7.8 %copy-start.1 = (bf16[16,6272]{1,0:T(8,128)(2,1)S(1)}, bf16[16,6272]{1,0:T(8,128)(2,1)}, u32[]{:S(2)}) copy-start(bf16[16,6272]{1,0:T(8,128)(2,1)} %param.7) | copy-start | bytes 602116
  4.6 52.3 %collective-permute-start = (f32[17,128]{1,0:T(8,128)S(1)}, f32[17,128]{1,0:T(8,128)S(1)}, u32[]{:S(2)}, u32[]{:S(2)}) collective-permute-start(f32[17,128]{1,0:T(8,128)S(1)} %get-tuple-element.16), channel_id=1, source_target_pairs={{0,1},{1,2},{2,3},{3,4},{4,5},{5,6},{6,7},{7,8},{8,9},{9,10},{10,1... | collective-permute-start | bytes 26120 | tf_op jit(solution)/shard_map/ppermute | solution.py:14
  9.4 47.5 %collective-permute-start.1 = (f32[17,128]{1,0:T(8,128)S(1)}, f32[17,128]{1,0:T(8,128)S(1)}, u32[]{:S(2)}, u32[]{:S(2)}) collective-permute-start(f32[17,128]{1,0:T(8,128)S(1)} %get-tuple-element.15), channel_id=1, source_target_pairs={{1,0},{2,1},{3,2},{4,3},{5,4},{6,5},{7,6},{8,7},{9,8},{10,9},{11,1... | collective-permute-start | bytes 26120 | tf_op jit(solution)/shard_map/ppermute | solution.py:15
  41.9 31.0 %all-to-all-start = ((f32[16,16,392]{2,1,0:T(8,128)}), f32[16,16,392]{2,1,0:T(8,128)S(1)}, u32[]{:S(2)}, u32[]{:S(2)}) async-start(f32[16,16,392]{2,1,0:T(8,128)} %bitcast.21), calls=%async_computation | async-start | bytes 1048576 | tf_op jit(solution)/shard_map/all_to_all | solution.py:88

commit v3 on v2

--- a/solution.py
+++ b/solution.py
@@ -84,19 +84,18 @@
     chunk = slots // count
     me = lax.axis_index(DP)
     first = me * chunk
-    pieces = partial_cells.reshape(nvecs, count, chunk).transpose(1, 0, 2)
-    pieces = lax.all_to_all(pieces, DP, 0, 0)
-    misfit = pieces[0]
+    pieces = partial_cells.reshape(nvecs, count, chunk)
+    pieces = lax.all_to_all(pieces, DP, 1, 1)
+    misfit = pieces[:, 0]
     for source in range(1, count):
-        misfit = misfit + pieces[source]
+        misfit = misfit + pieces[:, source]
     weight = jnp.where(live, depth_weight, jnp.float32(0.0))
     masked_f = masked.astype(jnp.float32)
     smooth = smooth_chunk(masked_f, weight, send_lists, neighbours, first, chunk)
     total = misfit + 0.5 * smooth
     live_chunk = lax.dynamic_slice_in_dim(live, first, chunk, axis=0)
     product = jnp.where(live_chunk[None, :], total, jnp.float32(0.0))
-    gathered = lax.all_gather(product, DP, axis=0)
-    return gathered.transpose(1, 0, 2).reshape(nvecs, slots)
+    return lax.all_gather(product, DP, axis=1, tiled=True)
 
 
 DP = ("y", "core")

time: 90.7 us -> 90.7 us (level)
    reshape x3 -> x2, local copies, waits for them, and re-layouts: 2.65 us -> 1.61 us  [on_device_body(): pieces = partial_cells.reshape(nvecs, count, chunk)]
    unnamed x7 -> x8, local copies, waits for them, and re-layouts: 0.34 us -> 1.39 us
where the time goes in v3:
time: 90.7 us; the launch traced here: 90.3 us
  blocking collectives  44.5 us (49%)
  starting transfers between devices  19.9 us (22%)
  waiting for transfers between devices  14.9 us (16%)
  local copies, waits for them, and re-layouts  3.52 us (4%)
  matrix products  3.23 us (4%)
  other arithmetic  3.2 us (4%)
  between operations  0.98 us (1%)
    psum x2, blocking collectives, on_device_body(): summed = lax.psum(lax.psum(partial_data, 'z'), 'x')  28.6 us
    all_gather x1, blocking collectives, on_device_body(): return lax.all_gather(product, DP, axis=1, tiled=True)  15.9 us
    all_to_all x1, waiting for transfers between devices, on_device_body(): pieces = lax.all_to_all(pieces, DP, 1, 1)  14.9 us
    all_to_all x1, starting transfers between devices, on_device_body(): pieces = lax.all_to_all(pieces, DP, 1, 1)  13.8 us
    ppermute x1, starting transfers between devices, padded_2(): before = lax.ppermute(last, axis, up)  4.81 us
  transfers between devices with their start and end apart: 3, of which 1 were waited for; matrix products, arithmetic and copies ran while one was open for 5% of the time, Pallas kernels for 0%

profile of v3, /device:TPU:1, one launch (start us, length us, event | category | flops | bytes accessed | tf_op | source)
XLA Modules:
  0.0 90.3 jit_solution(10005060051113930047)
XLA Ops:
  0.0 0.0 copy-start
  0.8 0.8 broadcast_select_fusion.2
  1.6 1.0 %broadcast_multiply_fusion = f32[16,6272]{1,0:T(8,128)S(1)} fusion(f32[6272]{0:T(1024)S(1)} %broadcast_select_fusion.2, bf16[16,6272]{1,0:T(8,128)(2,1)} %param.7, pred[6272]{0:T(1024)(128)(4,1)S(1)} %iota_compare_fusion.8), kind=kLoop, calls=%fused_computation.20 | loop fusion | flops 301056 | bytes 633472 | tf_op jit(solution)/shard_map/mul | solution.py:42
  2.6 0.0 copy-start.2
  2.6 0.1 reduce-precision_convert_fusion.1
  2.7 0.2 pad_maximum_fusion
  2.9 0.0 copy-start.1
  2.9 0.3 copy-done.2
  3.2 1.3 %fusion = f32[51,256]{1,0:T(8,128)S(1)} fusion(bf16[51,6272]{1,0:T(8,128)(2,1)S(1)} %pad_maximum_fusion, s32[256]{0:T(256)S(1)} %bitcast.32), kind=kOutput, calls=%fused_computation.1 | convolution fusion | flops 165380096 | bytes 692992 | tf_op jit(solution)/shard_map/dot_general | solution.py:33
  4.6 4.8 %collective-permute-start = (f32[17,128]{1,0:T(8,128)S(1)}, f32[17,128]{1,0:T(8,128)S(1)}, u32[]{:S(2)}, u32[]{:S(2)}) collective-permute-start(f32[17,128]{1,0:T(8,128)S(1)} %get-tuple-element.16), channel_id=1, source_target_pairs={{0,1},{1,2},{2,3},{3,4},{4,5},{5,6},{6,7},{7,8},{8,9},{9,10},{10,1... | collective-permute-start | bytes 26120 | tf_op jit(solution)/shard_map/ppermute | solution.py:14
  9.4 1.3 %collective-permute-start.1 = (f32[17,128]{1,0:T(8,128)S(1)}, f32[17,128]{1,0:T(8,128)S(1)}, u32[]{:S(2)}, u32[]{:S(2)}) collective-permute-start(f32[17,128]{1,0:T(8,128)S(1)} %get-tuple-element.15), channel_id=1, source_target_pairs={{1,0},{2,1},{3,2},{4,3},{5,4},{6,5},{7,6},{8,7},{9,8},{10,9},{11,1... | collective-permute-start | bytes 26120 | tf_op jit(solution)/shard_map/ppermute | solution.py:15
  10.7 0.0 copy-done
  10.7 0.0 copy-done.1
  10.7 0.5 fusion.5
  11.2 20.1 %psum.14 = f32[16,128]{1,0:T(8,128)S(1)} all-reduce(f32[16,128]{1,0:T(8,128)S(1)} %fusion.5), channel_id=1, replica_groups=mesh['y'=8,'core'=2,'x'=4,'z'=8] {'z'}, use_global_device_ids=true, to_apply=%region_0.1 | all-reduce | flops 2048 | bytes 16384 | tf_op jit(solution)/shard_map/psum | solution.py:77
  31.3 8.5 %psum.15 = f32[16,128]{1,0:T(8,128)S(1)} all-reduce(f32[16,128]{1,0:T(8,128)S(1)} %psum.14), channel_id=1, replica_groups=mesh['y'=8,'core'=2,'x'=4,'z'=8] {'x'}, use_global_device_ids=true, to_apply=%region_1.2 | all-reduce | flops 2048 | bytes 16384 | tf_op jit(solution)/shard_map/psum | solution.py:77
  39.9 0.3 fusion.22
  40.3 0.5 reshape.17
  40.8 1.1 %copy.10 = f32[16,16,392]{2,0,1:T(8,128)} copy(f32[16,16,392]{2,1,0:T(8,128)S(1)} %reshape.17) | data formatting | bytes 802816 | tf_op jit(solution)/shard_map/reshape | solution.py:87
  41.9 13.8 %all-to-all-start = ((f32[16,16,392]{2,0,1:T(8,128)}), f32[16,16,392]{2,0,1:T(8,128)S(1)}, u32[]{:S(2)}, u32[]{:S(2)}) async-start(f32[16,16,392]{2,0,1:T(8,128)} %copy.10), calls=%async_computation | async-start | bytes 1048576 | tf_op jit(solution)/shard_map/all_to_all | solution.py:88
  55.7 0.1 fusion.4
  55.8 0.1 pad_dynamic-slice_fusion
  55.9 0.8 select_select_fusion
  56.7 0.1 fusion.29
  56.8 0.1 dynamic_slice.15
  56.9 0.0 collective-permute-done
  56.9 0.0 collective-permute-done.1
  56.9 1.1 %fusion.2 = f32[51,392]{1,0:T(8,128)S(1)} fusion(s32[392]{0:T(512)S(1)} %bitcast.27, s32[392]{0:T(512)S(1)} %bitcast.28, s32[392]{0:T(512)S(1)} %bitcast.29, s32[392]{0:T(512)S(1)} %bitcast.30, s32[392]{0:T(512)S(1)} %bitcast.31, s32[392]{0:T(512)S(1)} %bitcast.26, bf16[17,256]{1,0:T(8,128)(2,1)S(1)} %get-tuple-element.13, ...), kind=kOutput, calls=%fused_computation.14 | convolution fusion | flops 36819648 | bytes 168528 | tf_op jit(solution)/shard_map/dot_general | solution.py:61
  58.1 14.9 %all-to-all-done = f32[16,16,392]{2,0,1:T(8,128)S(1)} async-done(((f32[16,16,392]{2,0,1:T(8,128)}), f32[16,16,392]{2,0,1:T(8,128)S(1)}, u32[]{:S(2)}, u32[]{:S(2)}) %all-to-all-start) | async-done | bytes 401440 | tf_op jit(solution)/shard_map/all_to_all | solution.py:88
  72.9 0.1 fusion.19
  73.0 15.9 %all-gather = f32[16,392,16]{1,2,0:T(8,128)S(1)} all-gather(f32[1,392,16]{1,2,0:T(8,128)S(1)} %fusion.19), channel_id=1, replica_groups=mesh['y'=8,'core'=2,'x'=4,'z'=8] {'y','core'}, dimensions={0}, use_global_device_ids=true | all-gather | bytes 426496 | tf_op jit(solution)/shard_map/all_gather | solution.py:98
  88.9 0.3 copy.11
  89.2 1.0 %reshape.27 = f32[6272,16]{0,1:T(8,128)} reshape(f32[16,392,16]{1,0,2:T(8,128)S(1)} %copy.11) | data formatting | bytes 802816
  (12 shorter events, 0.1 us)
Async XLA Ops:
  0.0 10.7 %copy-start = (bf16[128,6272]{1,0:T(8,128)(2,1)S(1)}, bf16[128,6272]{1,0:T(8,128)(2,1)}, u32[]{:S(2)}) copy-start(bf16[128,6272]{1,0:T(8,128)(2,1)} %param.6) | copy-start | bytes 4816900
  2.6 0.7 copy-start.2
  2.9 7.8 %copy-start.1 = (bf16[16,6272]{1,0:T(8,128)(2,1)S(1)}, bf16[16,6272]{1,0:T(8,128)(2,1)}, u32[]{:S(2)}) copy-start(bf16[16,6272]{1,0:T(8,128)(2,1)} %param.7) | copy-start | bytes 602116
  4.6 52.3 %collective-permute-start = (f32[17,128]{1,0:T(8,128)S(1)}, f32[17,128]{1,0:T(8,128)S(1)}, u32[]{:S(2)}, u32[]{:S(2)}) collective-permute-start(f32[17,128]{1,0:T(8,128)S(1)} %get-tuple-element.16), channel_id=1, source_target_pairs={{0,1},{1,2},{2,3},{3,4},{4,5},{5,6},{6,7},{7,8},{8,9},{9,10},{10,1... | collective-permute-start | bytes 26120 | tf_op jit(solution)/shard_map/ppermute | solution.py:14
  9.4 47.5 %collective-permute-start.1 = (f32[17,128]{1,0:T(8,128)S(1)}, f32[17,128]{1,0:T(8,128)S(1)}, u32[]{:S(2)}, u32[]{:S(2)}) collective-permute-start(f32[17,128]{1,0:T(8,128)S(1)} %get-tuple-element.15), channel_id=1, source_target_pairs={{1,0},{2,1},{3,2},{4,3},{5,4},{6,5},{7,6},{8,7},{9,8},{10,9},{11,1... | collective-permute-start | bytes 26120 | tf_op jit(solution)/shard_map/ppermute | solution.py:15
  41.9 31.0 %all-to-all-start = ((f32[16,16,392]{2,0,1:T(8,128)}), f32[16,16,392]{2,0,1:T(8,128)S(1)}, u32[]{:S(2)}, u32[]{:S(2)}) async-start(f32[16,16,392]{2,0,1:T(8,128)} %copy.10), calls=%async_computation | async-start | bytes 1048576 | tf_op jit(solution)/shard_map/all_to_all | solution.py:88
